TPU v7x, 32 devices: a whole 2x2x4 slice. The times are simulated.
32 devices in a mesh: groups: 2 (over y), prompt: 4 (over z), enc: 4 (over x, core).
Axes of the slice: x: 2, y: 2, z: 4, core: 2. Of those that a mesh axis runs over, the one named last changes fastest.
Arguments:
- embed: bfloat16 [8192, 256], P(('groups', 'prompt', 'enc')), parts along dimension 0, may hold values from -4000 to 4000
- coords: int32 [64, 6], P(('groups', 'prompt')), parts along dimension 0, may hold values from 0 to 1023
- targets: int32 [64], P(('groups', 'prompt')), parts along dimension 0, may hold values from 0 to 7
- counts: int32 [4], replicated, may hold values from 1 to 8, 16 in all
- labels: int32 [512, 256], P('groups'), parts along dimension 0, may hold values from 0 to 7
- type_embed: float32 [4, 256], replicated, may hold values from -5 to 5
- fourier: float32 [2, 128], replicated, may hold values from -5 to 5
- wq_t: bfloat16 [256, 128], replicated, may hold values from -0.375 to 0.375
- wk_t: bfloat16 [256, 128], replicated, may hold values from -0.375 to 0.375
- wv_t: bfloat16 [256, 128], replicated, may hold values from -0.375 to 0.375
- wo_t: bfloat16 [128, 256], replicated, may hold values from -0.5 to 0.5
- wq_i: bfloat16 [256, 128], replicated, may hold values from -0.375 to 0.375
- wk_i: bfloat16 [256, 128], replicated, may hold values from -0.375 to 0.375
- wv_i: bfloat16 [256, 128], replicated, may hold values from -0.375 to 0.375
- wo_i: bfloat16 [128, 256], replicated, may hold values from -0.5 to 0.5
- gain_one: float32 [256], replicated, may hold values from 0.1 to 1.9
- gain_two: float32 [256], replicated, may hold values from 0.1 to 1.9
- gain_three: float32 [64], replicated, may hold values from 0.1 to 1.9
- up_one: bfloat16 [256, 256], replicated, may hold values from -0.375 to 0.375
- second_upsample_weight: bfloat16 [64, 128], replicated, may hold values from -0.75 to 0.75
- hyper_one: bfloat16 [256, 256], replicated, may hold values from -0.375 to 0.375
- hyper_two: bfloat16 [256, 32], replicated, may hold values from -0.375 to 0.375
Outputs:
- grad_embed: float32 [8192, 256], P(('groups', 'prompt', 'enc')), parts along dimension 0
There are 2 independent parts, one for each index of `groups`. A program takes and returns all parts, laid end to end along the dimension named above; an argument that names none is the same for every part. Nothing has to cross between parts.
Inputs may be any that keep to these rules, and one draw needn't show every extreme that they name: Prompt index p has counts[p] live prompts, in its first slots; the counts sum to 16 and the largest is 8.
All inputs are finite; a program needn't handle non-finite values.
Results may differ from a plain program's by a relative error of at most 0.0035.
Values may be sent and summed in bfloat16 or wider, within the bound.
No kernel may reach another device: no remote copies, remote signals or barrier semaphores. Data moves between devices by JAX's collectives and lax.ppermute only.
A program may use at most 128 MiB of HBM per device.

v0:
```python
import math

import jax
import jax.numpy as jnp
from jax import lax
from jax.sharding import PartitionSpec as P

HEADS = 8
HD = 16
IMG = 1024


highest_value = lax.Precision.HIGHEST
epsilon = 1e-05


def joined(array, axis, combine):
    everything = jax.tree.map(lambda part: lax.all_gather(part, axis), array)
    leading = jax.tree.map(lambda part: part[0], everything)

    def step(k, so_far):
        return combine(so_far, jax.tree.map(lambda part: part[k], everything))

    return lax.fori_loop(1, lax.axis_size(axis), step, leading)


def layer_norm(values, gain):
    centered = values - jnp.mean(values, axis=-1, keepdims=True)
    variance = jnp.mean(centered * centered, axis=-1, keepdims=True)
    return centered * lax.rsqrt(variance + epsilon) * gain


def fourier_code(pixel_pair, fourier):
    scaled = 2.0 * ((pixel_pair.astype(jnp.float32) + 0.5) / IMG) - 1.0
    angles = 2.0 * math.pi * jnp.dot(scaled, fourier, precision=highest_value)
    return jnp.concatenate([jnp.sin(angles), jnp.cos(angles)], axis=-1)


def prompt_tokens(corner_rows, type_embed, fourier):
    point_code = fourier_code(corner_rows[..., 0:2], fourier) + type_embed[1]
    first_code = fourier_code(corner_rows[..., 2:4], fourier) + type_embed[2]
    second_code = fourier_code(corner_rows[..., 4:6], fourier) + type_embed[3]
    output_token = jnp.broadcast_to(type_embed[0], point_code.shape)
    return jnp.stack([output_token, point_code, first_code, second_code], axis=-2)


def token_pixel_scores(labels):
    side = labels.shape[0] // 4
    grid_view = labels.reshape(side, 2, 2, side, 2, 2)
    grid_view = jnp.transpose(grid_view, (0, 3, 1, 4, 2, 5))
    return grid_view.reshape(side * side, 4, 4)


def combine_parts(first, second_result):
    top_first, first_running_total, accum_first = first
    top_second, total_second, accum_second = second_result
    top_both = jnp.maximum(top_first, top_second)
    factor_first = jnp.exp(top_first - top_both)
    factor_second = jnp.exp(top_second - top_both)
    total_both = first_running_total * factor_first + total_second * factor_second
    accum_both = accum_first * factor_first[..., None] + accum_second * factor_second[..., None]
    return (top_both, total_both, accum_both)


def image_side(query_image, image_float, tokens_one, truth, live_flag, side_weights):
    wk_i, wv_i, wo_i, gain_two, up_one, gain_three, second_upsample_weight, hyper_one, hyper_two = (
        side_weights
    )
    head_scale = HD ** (-0.5)
    row_count = query_image.shape[0]
    token_keys = jnp.dot(tokens_one, wk_i.astype(jnp.float32), precision=highest_value).reshape(
        -1, HEADS, HD
    )
    token_values = jnp.dot(tokens_one, wv_i.astype(jnp.float32), precision=highest_value).reshape(
        -1, HEADS, HD
    )
    scores = (
        jnp.einsum(
            "jhd,rhd->jhr",
            query_image.reshape(row_count, HEADS, HD),
            token_keys,
            precision=highest_value,
        )
        * head_scale
    )
    attention = jax.nn.softmax(scores, axis=-1)
    mixed = (
        jnp.einsum("jhr,rhd->jhd", attention, token_values, precision=highest_value)
        .reshape(row_count, -1)
        .astype(jnp.bfloat16)
    )
    update = jnp.dot(mixed, wo_i, preferred_element_type=jnp.float32)
    image_one = layer_norm(image_float + update, gain_two).astype(jnp.bfloat16)
    lifted = jnp.dot(image_one, up_one, preferred_element_type=jnp.float32).reshape(
        row_count, 4, -1
    )
    first_activation = jax.nn.gelu(layer_norm(lifted, gain_three), approximate=False).astype(
        jnp.bfloat16
    )
    second_result = jnp.einsum(
        "oij,jp->oip", first_activation, second_upsample_weight, preferred_element_type=jnp.float32
    )
    features = jax.nn.gelu(second_result, approximate=False).reshape(row_count, 4, 4, -1)
    hidden = jax.nn.relu(
        jnp.dot(tokens_one[0], hyper_one.astype(jnp.float32), precision=highest_value)
    )
    hyper = jnp.dot(hidden, hyper_two.astype(jnp.float32), precision=highest_value)
    logits = jnp.einsum("tasc,c->tas", features, hyper, precision=highest_value)
    losses = jax.nn.softplus(logits) - truth * logits
    return jnp.sum(losses) * live_flag * 0.25


def on_device(
    embed,
    coords,
    targets,
    counts,
    labels,
    type_embed,
    fourier,
    wq_t,
    wk_t,
    wv_t,
    wo_t,
    wq_i,
    wk_i,
    wv_i,
    wo_i,
    gain_one,
    gain_two,
    gain_three,
    up_one,
    second_upsample_weight,
    hyper_one,
    hyper_two,
):
    prompt_count = lax.axis_size("prompt")
    enc_count = lax.axis_size("enc")
    prompt_place = lax.axis_index("prompt")
    enc_place = lax.axis_index("enc")
    block_rows = embed.shape[0]
    slot_count = coords.shape[0]
    head_scale = HD ** (-0.5)
    image = lax.all_gather(embed, "prompt", axis=0, tiled=True)
    image_float = image.astype(jnp.float32)
    key_image = jnp.dot(image, wk_t, preferred_element_type=jnp.float32)
    value_image = jnp.dot(image, wv_t, preferred_element_type=jnp.float32)
    query_image = jnp.dot(image, wq_i, preferred_element_type=jnp.float32)
    local_rows = image.shape[0]
    pixel_all = token_pixel_scores(labels).reshape(prompt_count, enc_count, block_rows, 4, 4)
    own_pixels = lax.dynamic_index_in_dim(pixel_all, enc_place, axis=1, keepdims=False).reshape(
        local_rows, 4, 4
    )
    own_count = jnp.take(counts, prompt_place)
    live_flags = (jnp.arange(slot_count, dtype=jnp.int32) < own_count).astype(jnp.float32)
    tokens_zero = prompt_tokens(coords, type_embed, fourier)
    prompt_number = tokens_zero.shape[0]
    flat_tokens = tokens_zero.reshape(prompt_number * 4, -1)
    queries = jnp.dot(flat_tokens, wq_t.astype(jnp.float32), precision=highest_value).reshape(
        -1, HEADS, HD
    )
    key_heads = key_image.reshape(local_rows, HEADS, HD)
    value_heads = value_image.reshape(local_rows, HEADS, HD)
    scores = jnp.einsum("rhd,jhd->rhj", queries, key_heads, precision=highest_value) * head_scale
    local_top = jnp.max(scores, axis=-1)
    shifted = jnp.exp(scores - local_top[..., None])
    local_total = jnp.sum(shifted, axis=-1)
    local_accum = jnp.einsum("rhj,jhd->rhd", shifted, value_heads, precision=highest_value)
    global_top, global_total, global_accum = joined(
        (local_top, local_total, local_accum), "enc", combine_parts
    )
    gathered = global_accum / global_total[..., None]
    wo_t_float = wo_t.astype(jnp.float32)
    update = jnp.dot(gathered.reshape(prompt_number * 4, -1), wo_t_float, precision=highest_value)

    def token_norm(values):
        return layer_norm(values, gain_one)

    tokens_one, norm_pull = jax.vjp(token_norm, flat_tokens + update)
    side_weights = (
        wk_i,
        wv_i,
        wo_i,
        gain_two,
        up_one,
        gain_three,
        second_upsample_weight,
        hyper_one,
        hyper_two,
    )

    def single_prompt(carry, inputs):
        tokens_row, target, live_flag = inputs
        truth = (own_pixels == target).astype(jnp.float32)

        def loss_of(query_arg, image_arg, tokens_arg):
            return image_side(query_arg, image_arg, tokens_arg, truth, live_flag, side_weights)

        _, pullback = jax.vjp(loss_of, query_image, image_float, tokens_row)
        d_query, d_image, d_tokens = pullback(jnp.ones((), jnp.float32))
        return ((carry[0] + d_query, carry[1] + d_image), d_tokens)

    initial = (jnp.zeros_like(query_image), jnp.zeros_like(image_float))
    sums, token_parts = lax.scan(
        single_prompt, initial, (tokens_one.reshape(prompt_number, 4, -1), targets, live_flags)
    )
    query_grad, image_grad = sums
    token_grad = lax.psum(token_parts, "enc")
    (d_residual,) = norm_pull(token_grad.reshape(prompt_number * 4, -1))
    d_gathered = jnp.dot(d_residual, wo_t_float.T, precision=highest_value).reshape(-1, HEADS, HD)
    probs = jnp.exp(scores - global_top[..., None]) / global_total[..., None]
    d_probs = jnp.einsum("rhd,jhd->rhj", d_gathered, value_heads, precision=highest_value)
    delta_term = jnp.sum(d_gathered * gathered, axis=-1)
    d_scores = probs * (d_probs - delta_term[..., None]) * head_scale
    key_grad = jnp.einsum("rhj,rhd->jhd", d_scores, queries, precision=highest_value).reshape(
        local_rows, -1
    )
    value_grad = jnp.einsum("rhj,rhd->jhd", probs, d_gathered, precision=highest_value).reshape(
        local_rows, -1
    )
    wq_i_float = wq_i.astype(jnp.float32)
    wk_t_float = wk_t.astype(jnp.float32)
    wv_t_float = wv_t.astype(jnp.float32)
    result = image_grad
    result = result + jnp.dot(query_grad, wq_i_float.T, precision=highest_value)
    result = result + jnp.dot(key_grad, wk_t_float.T, precision=highest_value)
    result = result + jnp.dot(value_grad, wv_t_float.T, precision=highest_value)
    summed = lax.psum(result, "prompt")
    grad_embed = lax.dynamic_slice_in_dim(summed, prompt_place * block_rows, block_rows, 0)
    return grad_embed


def solution(mesh):
    in_specs = (
        P(("groups", "prompt", "enc"), None),
        P(("groups", "prompt"), None),
        P(("groups", "prompt")),
        P(),
        P("groups", None),
        P(),
        P(),
        P(),
        P(),
        P(),
        P(),
        P(),
        P(),
        P(),
        P(),
        P(),
        P(),
        P(),
        P(),
        P(),
        P(),
        P(),
    )
    out_specs = P(("groups", "prompt", "enc"), None)
    return jax.shard_map(
        on_device, mesh=mesh, in_specs=in_specs, out_specs=out_specs, check_vma=False
    )
```

profile of v0, /device:TPU:0, one launch (start us, length us, event | category | flops | bytes accessed | tf_op | source)
XLA Modules:
  0.0 566.2 jit_solution(3963014833679820841)
XLA Ops:
  12.3 17.4 %all_gather.21 = bf16[1024,256]{0,1:T(8,128)(2,1)S(1)} all-gather(bf16[256,256]{0,1:T(8,128)(2,1)S(1)} %copy.50), channel_id=1, replica_groups=mesh['groups'=2,'prompt'=4,'enc'=4] {'prompt'}, dimensions={0}, use_global_device_ids=true | all-gather | bytes 655360 | tf_op jit(solution)/shard_map/all_gather | solution.py:144
  33.9 7.2 %all-gather.2 = f32[128,8,16]{2,1,0:T(8,128)S(1)} all-gather(f32[32,8,16]{2,1,0:T(8,128)S(1)} %copy.52), channel_id=4, replica_groups=mesh['groups'=2,'prompt'=4,'enc'=4] {'enc'}, dimensions={0}, use_global_device_ids=true | all-gather | bytes 81920 | tf_op jit(solution)/shard_map/all_gather | solution.py:18
  41.4 5.2 all-gather.4
  46.6 5.2 all-gather.3
  55.4 27.0 %reshape.331 = s32[64,2,2,64,2,2]{5,4,3,2,1,0:T(2,128)} reshape(s32[256,256]{1,0:T(8,128)S(1)} %copy-done.55) | data formatting | bytes 524288 | tf_op jit(solution)/shard_map/reshape | solution.py:49
  82.4 20.9 %copy.55 = s32[64,64,2,2,2,2]{1,0,5,4,3,2:T(8,128)S(1)} copy(s32[64,64,2,2,2,2]{5,3,1,4,2,0:T(2,128)} %bitcast.446) | data formatting | bytes 524288 | tf_op jit(solution)/shard_map/transpose | solution.py:50
  105.7 374.7 %while.36 = (s32[]{:T(128)}, f32[1024,128]{0,1:T(8,128)}, f32[1024,256]{0,1:T(8,128)}, f32[8,4,256]{2,1,0:T(4,128)}, f32[8,4,256]{2,1,0:T(4,128)}, /*index=5*/bf...) while((s32[]{:T(128)}, f32[1024,128]{0,1:T(8,128)}, ...), condition=%wide.region_18.19_spmd.clone, body=%wide.region_6.18_spmd.clone.sunk | while | flops 692868864 | bytes 118107712 | solution.py:204
  112.7 3.8 fusion.345
  116.6 5.5 multiply_multiply_fusion.19
  123.1 1.9 fusion.346
  129.5 2.7 fusion.348
  132.2 3.6 multiply_reduce_fusion.13
  148.7 1.9 fusion.352
  158.6 3.8 fusion.345
  162.5 5.5 multiply_multiply_fusion.19
  169.0 1.9 fusion.346
  175.4 2.7 fusion.348
  178.0 3.6 multiply_reduce_fusion.13
  194.6 1.9 fusion.352
  196.5 1.9 bitcast_add_fusion.2
  205.6 3.8 fusion.345
  209.4 5.5 multiply_multiply_fusion.19
  216.0 1.9 fusion.346
  222.3 2.7 fusion.348
  225.0 3.6 multiply_reduce_fusion.13
  241.6 1.9 fusion.352
  243.5 1.9 bitcast_add_fusion.2
  252.5 3.8 fusion.345
  256.3 5.5 multiply_multiply_fusion.19
  262.9 1.9 fusion.346
  269.3 2.7 fusion.348
  271.9 3.6 multiply_reduce_fusion.13
  288.5 1.9 fusion.352
  290.4 1.9 bitcast_add_fusion.2
  299.4 3.8 fusion.345
  303.3 5.5 multiply_multiply_fusion.19
  309.9 1.9 fusion.346
  316.2 2.7 fusion.348
  318.9 3.6 multiply_reduce_fusion.13
  335.5 1.9 fusion.352
  337.4 1.9 bitcast_add_fusion.2
  346.4 3.8 fusion.345
  350.2 5.5 multiply_multiply_fusion.19
  356.8 1.9 fusion.346
  363.2 2.7 fusion.348
  365.8 3.6 multiply_reduce_fusion.13
  382.4 1.9 fusion.352
  384.3 1.9 bitcast_add_fusion.2
  393.3 3.8 fusion.345
  397.2 5.5 multiply_multiply_fusion.19
  410.1 2.7 fusion.348
  412.8 3.6 multiply_reduce_fusion.13
  429.4 1.9 fusion.352
  431.3 1.9 bitcast_add_fusion.2
  440.3 3.8 fusion.345
  444.1 5.5 multiply_multiply_fusion.19
  450.7 1.9 fusion.346
  457.0 2.7 fusion.348
  459.7 3.6 multiply_reduce_fusion.13
  476.3 1.9 fusion.352
  478.2 1.9 bitcast_add_fusion.2
  481.2 10.9 %psum.14 = f32[32,256]{1,0:T(8,128)S(1)} all-reduce(f32[32,256]{1,0:T(8,128)S(1)} %reshape.333), channel_id=1, replica_groups=mesh['groups'=2,'prompt'=4,'enc'=4] {'enc'}, use_global_device_ids=true, to_apply=%region_19.20 | all-reduce | flops 8192 | bytes 65536 | tf_op jit(solution)/shard_map/psum | solution.py:208
  496.0 2.1 fusion.118
  504.3 53.4 %all-reduce.3.cloned.1.call-done = f32[1024,256]{1,0:T(8,128)} async-done(((f32[1024,256]{1,0:T(8,128)}), f32[1024,256]{1,0:T(8,128)}) %all-reduce.3.cloned.1.call-update) | async-done | bytes 1048592 | tf_op jit(solution)/shard_map/psum | solution.py:228
  (1268 shorter events, 225.0 us)
Async XLA Ops:
  6.5 98.0 %copy-start = (bf16[256,128]{1,0:T(8,128)(2,1)S(1)}, bf16[256,128]{1,0:T(8,128)(2,1)}, u32[]{:S(2)}) copy-start(bf16[256,128]{1,0:T(8,128)(2,1)} %param.37) | copy-start | bytes 196612
  6.5 23.2 %copy-start.57 = (bf16[256,128]{1,0:T(8,128)(2,1)S(1)}, bf16[256,128]{1,0:T(8,128)(2,1)}, u32[]{:S(2)}) copy-start(bf16[256,128]{1,0:T(8,128)(2,1)} %param.34) | copy-start | bytes 196612
  6.5 23.5 %copy-start.59 = (bf16[256,128]{1,0:T(8,128)(2,1)S(1)}, bf16[256,128]{1,0:T(8,128)(2,1)}, u32[]{:S(2)}) copy-start(bf16[256,128]{1,0:T(8,128)(2,1)} %param.35) | copy-start | bytes 196612
  6.5 551.2 %all-reduce.3.cloned.1.call-start = ((), (), s32[]{:S(2)}) async-start(), calls=%async_computation | async-start | bytes 2097152 | tf_op jit(solution)/shard_map/psum | solution.py:228
  33.8 18.3 %copy-start.56 = (bf16[128,256]{1,0:T(8,128)(2,1)S(1)}, bf16[128,256]{1,0:T(8,128)(2,1)}, u32[]{:S(2)}) copy-start(bf16[128,256]{1,0:T(8,128)(2,1)} %param.36) | copy-start | bytes 196612
  33.8 19.2 %copy-start.70 = (f32[256]{0:T(256)S(1)}, f32[256]{0:T(256)}, u32[]{:S(2)}) copy-start(f32[256]{0:T(256)} %param.41) | copy-start | bytes 3076
  33.8 19.9 %copy-start.74 = (s32[4]{0:T(128)S(1)}, s32[4]{0:T(128)}, u32[]{:S(2)}) copy-start(s32[4]{0:T(128)} %param.29) | copy-start | bytes 52
  33.8 21.6 %copy-start.55 = (s32[256,256]{1,0:T(8,128)S(1)}, s32[256,256]{1,0:T(8,128)}, u32[]{:S(2)}) copy-start(s32[256,256]{1,0:T(8,128)} %param.30) | copy-start | bytes 786436
  52.0 30.4 %copy-start.63 = (f32[32,8]{0,1:T(8,128)}, f32[32,8]{0,1:T(8,128)S(1)}, u32[]{:S(2)}) copy-start(f32[32,8]{0,1:T(8,128)S(1)} %get-tuple-element.283) | copy-start | bytes 3076
  52.0 30.4 %copy-start.65 = (f32[32,8]{0,1:T(8,128)}, f32[32,8]{0,1:T(8,128)S(1)}, u32[]{:S(2)}) copy-start(f32[32,8]{0,1:T(8,128)S(1)} %get-tuple-element.286) | copy-start | bytes 3076
  52.0 30.4 %copy-start.52 = (f32[32,8,16]{0,2,1:T(8,128)}, f32[32,8,16]{0,2,1:T(8,128)S(1)}, u32[]{:S(2)}) copy-start(f32[32,8,16]{0,2,1:T(8,128)S(1)} %broadcast_divide_fusion) | copy-start | bytes 49156
  52.4 30.0 %copy-start.71 = (f32[32]{0:T(128)}, f32[32]{0:T(128)S(1)}, u32[]{:S(2)}) copy-start(f32[32]{0:T(128)S(1)} %broadcast_multiply_fusion.3) | copy-start | bytes 388
  52.6 29.8 %copy-start.73 = (f32[32]{0:T(128)}, f32[32]{0:T(128)S(1)}, u32[]{:S(2)}) copy-start(f32[32]{0:T(128)S(1)} %multiply_reduce_fusion.6) | copy-start | bytes 388
  53.0 29.5 %copy-start.72 = (f32[32]{0:T(128)}, f32[32]{0:T(128)S(1)}, u32[]{:S(2)}) copy-start(f32[32]{0:T(128)S(1)} %fusion.146) | copy-start | bytes 388
  105.7 4.9 copy-start.7
  105.7 5.0 copy-start.22
  116.5 5.6 copy-start.5
  116.5 5.6 copy-start.18
  116.5 6.4 %copy-start.53 = (bf16[256,32]{0,1:T(8,128)(2,1)S(1)}, bf16[256,32]{0,1:T(8,128)(2,1)}, u32[]{:S(2)}) copy-start(bf16[256,32]{0,1:T(8,128)(2,1)} %get-tuple-element.825) | copy-start | bytes 49156 | tf_op jit(solution)/shard_map/while
  141.7 6.0 %copy-start.4 = (f32[1024,256]{0,1:T(8,128)S(1)}, f32[1024,256]{0,1:T(8,128)}, u32[]{:S(2)}) copy-start(f32[1024,256]{0,1:T(8,128)} %copy-done.3) | copy-start | bytes 3145732 | tf_op jit(solution)/shard_map/while
  151.6 4.9 copy-start.7
  151.6 4.9 copy-start.22
  162.4 5.6 copy-start.5
  162.4 5.6 copy-start.18
  162.4 6.4 %copy-start.53 = (bf16[256,32]{0,1:T(8,128)(2,1)S(1)}, bf16[256,32]{0,1:T(8,128)(2,1)}, u32[]{:S(2)}) copy-start(bf16[256,32]{0,1:T(8,128)(2,1)} %get-tuple-element.825) | copy-start | bytes 49156 | tf_op jit(solution)/shard_map/while
  187.5 6.0 %copy-start.4 = (f32[1024,256]{0,1:T(8,128)S(1)}, f32[1024,256]{0,1:T(8,128)}, u32[]{:S(2)}) copy-start(f32[1024,256]{0,1:T(8,128)} %copy-done.3) | copy-start | bytes 3145732 | tf_op jit(solution)/shard_map/while
  190.4 4.2 copy-start.40
  198.5 4.9 copy-start.7
  198.5 4.9 copy-start.22
  209.4 5.6 copy-start.5
  209.4 5.6 copy-start.18
  209.4 6.5 %copy-start.53 = (bf16[256,32]{0,1:T(8,128)(2,1)S(1)}, bf16[256,32]{0,1:T(8,128)(2,1)}, u32[]{:S(2)}) copy-start(bf16[256,32]{0,1:T(8,128)(2,1)} %get-tuple-element.825) | copy-start | bytes 49156 | tf_op jit(solution)/shard_map/while
  234.5 6.0 %copy-start.4 = (f32[1024,256]{0,1:T(8,128)S(1)}, f32[1024,256]{0,1:T(8,128)}, u32[]{:S(2)}) copy-start(f32[1024,256]{0,1:T(8,128)} %copy-done.3) | copy-start | bytes 3145732 | tf_op jit(solution)/shard_map/while
  245.5 4.9 copy-start.7
  245.5 4.9 copy-start.22
  256.3 5.6 copy-start.5
  256.3 5.6 copy-start.18
  256.3 6.5 %copy-start.53 = (bf16[256,32]{0,1:T(8,128)(2,1)S(1)}, bf16[256,32]{0,1:T(8,128)(2,1)}, u32[]{:S(2)}) copy-start(bf16[256,32]{0,1:T(8,128)(2,1)} %get-tuple-element.825) | copy-start | bytes 49156 | tf_op jit(solution)/shard_map/while
  281.5 6.0 %copy-start.4 = (f32[1024,256]{0,1:T(8,128)S(1)}, f32[1024,256]{0,1:T(8,128)}, u32[]{:S(2)}) copy-start(f32[1024,256]{0,1:T(8,128)} %copy-done.3) | copy-start | bytes 3145732 | tf_op jit(solution)/shard_map/while
  292.4 4.9 copy-start.7
  292.4 4.9 copy-start.22
  303.3 5.6 copy-start.5
  303.3 5.6 copy-start.18
  303.3 6.5 %copy-start.53 = (bf16[256,32]{0,1:T(8,128)(2,1)S(1)}, bf16[256,32]{0,1:T(8,128)(2,1)}, u32[]{:S(2)}) copy-start(bf16[256,32]{0,1:T(8,128)(2,1)} %get-tuple-element.825) | copy-start | bytes 49156 | tf_op jit(solution)/shard_map/while
  328.4 6.0 %copy-start.4 = (f32[1024,256]{0,1:T(8,128)S(1)}, f32[1024,256]{0,1:T(8,128)}, u32[]{:S(2)}) copy-start(f32[1024,256]{0,1:T(8,128)} %copy-done.3) | copy-start | bytes 3145732 | tf_op jit(solution)/shard_map/while
  339.3 4.9 copy-start.7
  339.4 4.9 copy-start.22
  350.2 5.6 copy-start.5
  350.2 5.6 copy-start.18
  350.2 6.5 %copy-start.53 = (bf16[256,32]{0,1:T(8,128)(2,1)S(1)}, bf16[256,32]{0,1:T(8,128)(2,1)}, u32[]{:S(2)}) copy-start(bf16[256,32]{0,1:T(8,128)(2,1)} %get-tuple-element.825) | copy-start | bytes 49156 | tf_op jit(solution)/shard_map/while
  375.3 6.0 %copy-start.4 = (f32[1024,256]{0,1:T(8,128)S(1)}, f32[1024,256]{0,1:T(8,128)}, u32[]{:S(2)}) copy-start(f32[1024,256]{0,1:T(8,128)} %copy-done.3) | copy-start | bytes 3145732 | tf_op jit(solution)/shard_map/while
  386.3 4.9 copy-start.7
  386.3 4.9 copy-start.22
  397.2 5.6 copy-start.5
  397.2 5.6 copy-start.18
  397.2 6.4 %copy-start.53 = (bf16[256,32]{0,1:T(8,128)(2,1)S(1)}, bf16[256,32]{0,1:T(8,128)(2,1)}, u32[]{:S(2)}) copy-start(bf16[256,32]{0,1:T(8,128)(2,1)} %get-tuple-element.825) | copy-start | bytes 49156 | tf_op jit(solution)/shard_map/while
  422.3 6.0 %copy-start.4 = (f32[1024,256]{0,1:T(8,128)S(1)}, f32[1024,256]{0,1:T(8,128)}, u32[]{:S(2)}) copy-start(f32[1024,256]{0,1:T(8,128)} %copy-done.3) | copy-start | bytes 3145732 | tf_op jit(solution)/shard_map/while
  425.2 4.2 copy-start.40
  433.2 4.9 copy-start.7
  433.3 4.9 copy-start.22
  444.1 5.6 copy-start.5
  444.1 5.6 copy-start.18
  444.1 6.4 %copy-start.53 = (bf16[256,32]{0,1:T(8,128)(2,1)S(1)}, bf16[256,32]{0,1:T(8,128)(2,1)}, u32[]{:S(2)}) copy-start(bf16[256,32]{0,1:T(8,128)(2,1)} %get-tuple-element.825) | copy-start | bytes 49156 | tf_op jit(solution)/shard_map/while
  469.2 6.0 %copy-start.4 = (f32[1024,256]{0,1:T(8,128)S(1)}, f32[1024,256]{0,1:T(8,128)}, u32[]{:S(2)}) copy-start(f32[1024,256]{0,1:T(8,128)} %copy-done.3) | copy-start | bytes 3145732 | tf_op jit(solution)/shard_map/while
  (357 other events, 860.2 us)
Sparse Core Ops, SparseCore 0:
  504.4 53.2 all-reduce.2
where the time goes:
time: 573 us; the launch traced here: 566 us
  matrix products  223 us (39%)
  other arithmetic  124 us (22%)
  local copies, waits for them, and re-layouts  95 us (17%)
  waiting for transfers between devices  53.4 us (9%)
  blocking collectives  45.8 us (8%)
  between operations  14.6 us (3%)
  loops' own time  11.1 us (2%)
    dot_general x16, matrix products, image_side(): jnp.einsum('oij,jp->oip', first_activation, second_upsample_weight, prefe...  59.2 us
    psum x1, waiting for transfers between devices, on_device(): summed = lax.psum(result, 'prompt')  53.4 us
    mul x8, other arithmetic, image_side(): jax.nn.gelu(second_result, approximate=False).reshape(row_count, 4, 4, -1)  44.4 us
    dot_general x16, matrix products, image_side(): logits = jnp.einsum('tasc,c->tas', features, hyper, precision=highest_value)  28.8 us
    reshape x1, local copies, waits for them, and re-layouts, token_pixel_scores(): grid_view = labels.reshape(side, 2, 2, side, 2, 2)  27 us
    dot_general x24, matrix products, image_side(): jnp.einsum('jhd,rhd->jhr', query_image.reshape(row_count, HEADS, HD), tok...  24.1 us
    dot_general x16, matrix products, image_side(): jnp.dot(tokens_one, wk_i.astype(jnp.float32), precision=highest_value)  23 us
    add x16, other arithmetic, single_prompt(): return ((carry[0] + d_query, carry[1] + d_image), d_tokens)  22.7 us
  transfers between devices with their start and end apart: 1, of which 1 were waited for; matrix products, arithmetic and copies ran while one was open for 0% of the time, Pallas kernels for 0%

commit v1 on v0

--- a/solution.py
+++ b/solution.py
@@ -134,6 +134,7 @@
     hyper_one,
     hyper_two,
 ):
+    both = ("prompt", "enc")
     prompt_count = lax.axis_size("prompt")
     enc_count = lax.axis_size("enc")
     prompt_place = lax.axis_index("prompt")
@@ -141,19 +142,27 @@
     block_rows = embed.shape[0]
     slot_count = coords.shape[0]
     head_scale = HD ** (-0.5)
-    image = lax.all_gather(embed, "prompt", axis=0, tiled=True)
-    image_float = image.astype(jnp.float32)
-    key_image = jnp.dot(image, wk_t, preferred_element_type=jnp.float32)
-    value_image = jnp.dot(image, wv_t, preferred_element_type=jnp.float32)
-    query_image = jnp.dot(image, wq_i, preferred_element_type=jnp.float32)
-    local_rows = image.shape[0]
-    pixel_all = token_pixel_scores(labels).reshape(prompt_count, enc_count, block_rows, 4, 4)
-    own_pixels = lax.dynamic_index_in_dim(pixel_all, enc_place, axis=1, keepdims=False).reshape(
-        local_rows, 4, 4
-    )
-    own_count = jnp.take(counts, prompt_place)
-    live_flags = (jnp.arange(slot_count, dtype=jnp.int32) < own_count).astype(jnp.float32)
-    tokens_zero = prompt_tokens(coords, type_embed, fourier)
+    live_total = prompt_count * slot_count // 2
+    chunk = math.gcd(live_total, max(1, 1024 // block_rows))
+    image_float = embed.astype(jnp.float32)
+    key_image = jnp.dot(embed, wk_t, preferred_element_type=jnp.float32)
+    value_image = jnp.dot(embed, wv_t, preferred_element_type=jnp.float32)
+    query_image = jnp.dot(embed, wq_i, preferred_element_type=jnp.float32)
+    local_rows = block_rows
+    pixel_all = token_pixel_scores(labels)
+    own_pixels = lax.dynamic_slice_in_dim(
+        pixel_all, (prompt_place * enc_count + enc_place) * block_rows, block_rows, 0
+    )
+    all_coords = lax.all_gather(coords, "prompt", axis=0, tiled=True)
+    all_targets = lax.all_gather(targets, "prompt", axis=0, tiled=True)
+    ends = jnp.cumsum(counts).astype(jnp.int32)
+    numbers = jnp.arange(live_total, dtype=jnp.int32)
+    owners = jnp.sum((ends[None, :] <= numbers[:, None]).astype(jnp.int32), axis=1)
+    starts = jnp.take(ends, owners) - jnp.take(counts, owners)
+    slot_index = (owners * slot_count + numbers - starts).astype(jnp.int32)
+    chosen_rows = jnp.take(all_coords, slot_index, axis=0)
+    chosen_targets = jnp.take(all_targets, slot_index)
+    tokens_zero = prompt_tokens(chosen_rows, type_embed, fourier)
     prompt_number = tokens_zero.shape[0]
     flat_tokens = tokens_zero.reshape(prompt_number * 4, -1)
     queries = jnp.dot(flat_tokens, wq_t.astype(jnp.float32), precision=highest_value).reshape(
@@ -163,12 +172,11 @@
     value_heads = value_image.reshape(local_rows, HEADS, HD)
     scores = jnp.einsum("rhd,jhd->rhj", queries, key_heads, precision=highest_value) * head_scale
     local_top = jnp.max(scores, axis=-1)
-    shifted = jnp.exp(scores - local_top[..., None])
+    global_top = lax.pmax(local_top, both)
+    shifted = jnp.exp(scores - global_top[..., None])
     local_total = jnp.sum(shifted, axis=-1)
     local_accum = jnp.einsum("rhj,jhd->rhd", shifted, value_heads, precision=highest_value)
-    global_top, global_total, global_accum = joined(
-        (local_top, local_total, local_accum), "enc", combine_parts
-    )
+    global_total, global_accum = lax.psum((local_total, local_accum), both)
     gathered = global_accum / global_total[..., None]
     wo_t_float = wo_t.astype(jnp.float32)
     update = jnp.dot(gathered.reshape(prompt_number * 4, -1), wo_t_float, precision=highest_value)
@@ -189,26 +197,37 @@
         hyper_two,
     )
 
-    def single_prompt(carry, inputs):
-        tokens_row, target, live_flag = inputs
+    def prompt_loss(query_arg, image_arg, tokens_row, target):
         truth = (own_pixels == target).astype(jnp.float32)
+        return image_side(query_arg, image_arg, tokens_row, truth, 1.0, side_weights)
+
+    def chunk_step(carry, inputs):
+        tokens_rows, chunk_targets = inputs
 
         def loss_of(query_arg, image_arg, tokens_arg):
-            return image_side(query_arg, image_arg, tokens_arg, truth, live_flag, side_weights)
-
-        _, pullback = jax.vjp(loss_of, query_image, image_float, tokens_row)
+            losses = jax.vmap(prompt_loss, in_axes=(None, None, 0, 0))(
+                query_arg, image_arg, tokens_arg, chunk_targets
+            )
+            return jnp.sum(losses)
+
+        _, pullback = jax.vjp(loss_of, query_image, image_float, tokens_rows)
         d_query, d_image, d_tokens = pullback(jnp.ones((), jnp.float32))
         return ((carry[0] + d_query, carry[1] + d_image), d_tokens)
 
     initial = (jnp.zeros_like(query_image), jnp.zeros_like(image_float))
     sums, token_parts = lax.scan(
-        single_prompt, initial, (tokens_one.reshape(prompt_number, 4, -1), targets, live_flags)
+        chunk_step,
+        initial,
+        (
+            tokens_one.reshape(prompt_number // chunk, chunk, 4, -1),
+            chosen_targets.reshape(prompt_number // chunk, chunk),
+        ),
     )
     query_grad, image_grad = sums
-    token_grad = lax.psum(token_parts, "enc")
+    token_grad = lax.psum(token_parts, both)
     (d_residual,) = norm_pull(token_grad.reshape(prompt_number * 4, -1))
     d_gathered = jnp.dot(d_residual, wo_t_float.T, precision=highest_value).reshape(-1, HEADS, HD)
-    probs = jnp.exp(scores - global_top[..., None]) / global_total[..., None]
+    probs = shifted / global_total[..., None]
     d_probs = jnp.einsum("rhd,jhd->rhj", d_gathered, value_heads, precision=highest_value)
     delta_term = jnp.sum(d_gathered * gathered, axis=-1)
     d_scores = probs * (d_probs - delta_term[..., None]) * head_scale
@@ -225,9 +244,7 @@
     result = result + jnp.dot(query_grad, wq_i_float.T, precision=highest_value)
     result = result + jnp.dot(key_grad, wk_t_float.T, precision=highest_value)
     result = result + jnp.dot(value_grad, wv_t_float.T, precision=highest_value)
-    summed = lax.psum(result, "prompt")
-    grad_embed = lax.dynamic_slice_in_dim(summed, prompt_place * block_rows, block_rows, 0)
-    return grad_embed
+    return result
 
 
 def solution(mesh):

time: 573 us -> 418 us (0.73)
  matrix products: 223 us -> 95.5 us
  other arithmetic: 124 us -> 36.3 us
  blocking collectives: 45.8 us -> 109 us
  waiting for transfers between devices: 53.4 us -> 84.1 us
  local copies, waits for them, and re-layouts: 95 us -> 72.1 us
  loops' own time: 11.1 us -> 1.4 us
    psum x1, blocking collectives: 10.9 us -> 58.4 us  [on_device(): global_total, global_accum = lax.psum((local_total, local_accum), both)]
    psum x1, waiting for transfers between devices: 53.4 us -> 84.1 us  [on_device(): token_grad = lax.psum(token_parts, both)]
    pmax x0 -> x1, blocking collectives: none -> 30.3 us  [on_device(): global_top = lax.pmax(local_top, both)]
    dot_general x16 -> x8, matrix products: 59.2 us -> 29.2 us  [image_side(): jnp.einsum('oij,jp->oip', first_activation, second_upsample_weight, prefe...]
    mul x8 -> x4, other arithmetic: 44.4 us -> 18.5 us  [image_side(): jax.nn.gelu(second_result, approximate=False).reshape(row_count, 4, 4, -1)]
    add x22 -> x8, other arithmetic: 22.8 us -> 0.4 us  [chunk_step(): return ((carry[0] + d_query, carry[1] + d_image), d_tokens)]
    dot_general x24 -> x12, matrix products: 24.1 us -> 4 us  [image_side(): jnp.einsum('jhd,rhd->jhr', query_image.reshape(row_count, HEADS, HD), tok...]
    while x787 -> x17, local copies, waits for them, and re-layouts: 21.5 us -> 1.48 us
where the time goes in v1:
time: 418 us; the launch traced here: 413 us
  blocking collectives  109 us (26%)
  matrix products  95.5 us (23%)
  waiting for transfers between devices  84.1 us (20%)
  local copies, waits for them, and re-layouts  72.1 us (17%)
  other arithmetic  36.3 us (9%)
  between operations  14.8 us (4%)
    psum x1, waiting for transfers between devices, on_device(): token_grad = lax.psum(token_parts, both)  84.1 us
    psum x1, blocking collectives, on_device(): global_total, global_accum = lax.psum((local_total, local_accum), both)  58.4 us
    pmax x1, blocking collectives, on_device(): global_top = lax.pmax(local_top, both)  30.3 us
    dot_general x8, matrix products, image_side(): jnp.einsum('oij,jp->oip', first_activation, second_upsample_weight, prefe...  29.2 us
    reshape x1, local copies, waits for them, and re-layouts, token_pixel_scores(): grid_view = labels.reshape(side, 2, 2, side, 2, 2)  27 us
    transpose x1, local copies, waits for them, and re-layouts, token_pixel_scores(): grid_view = jnp.transpose(grid_view, (0, 3, 1, 4, 2, 5))  21.1 us
    mul x4, other arithmetic, image_side(): jax.nn.gelu(second_result, approximate=False).reshape(row_count, 4, 4, -1)  18.5 us
    all_gather x1, blocking collectives, on_device(): all_coords = lax.all_gather(coords, 'prompt', axis=0, tiled=True)  14.9 us
  transfers between devices with their start and end apart: 1, of which 1 were waited for; matrix products, arithmetic and copies ran while one was open for 0% of the time, Pallas kernels for 0%

profile of v1, /device:TPU:0, one launch (start us, length us, event | category | flops | bytes accessed | tf_op | source)
XLA Modules:
  0.0 413.4 jit_solution(3780452449382497078)
XLA Ops:
  6.6 0.9 reduce-window.8
  8.2 1.3 gather_fusion.3
  9.6 14.9 %all_gather.6 = s32[32,6]{1,0:T(8,128)S(1)} all-gather(s32[8,6]{1,0:T(8,128)} %param.27), channel_id=1, replica_groups=mesh['groups'=2,'prompt'=4,'enc'=4] {'prompt'}, dimensions={0}, use_global_device_ids=true | all-gather | bytes 960 | tf_op jit(solution)/shard_map/all_gather | solution.py:156
  25.2 0.9 sine_bitcast_fusion.2
  26.1 1.0 sine_bitcast_fusion.1
  27.0 0.9 sine_bitcast_fusion
  29.1 0.9 copy.151
  31.9 30.3 %pmax.7 = f32[64,8]{0,1:T(8,128)S(1)} all-reduce(f32[64,8]{0,1:T(8,128)S(1)} %get-tuple-element.320), channel_id=1, replica_groups=mesh['groups'=2,'prompt'=4,'enc'=4] {'prompt','enc'}, use_global_device_ids=true, to_apply=%region_3.5 | all-reduce | flops 512 | bytes 4096 | tf_op jit(solution)/shard_map/pmax | solution.py:175
  63.5 58.4 %all-reduce.2 = (f32[64,8,16]{0,2,1:T(8,128)S(1)}, f32[64,8]{0,1:T(8,128)S(1)}) all-reduce(f32[64,8,16]{0,2,1:T(8,128)S(1)} %convolution_bitcast_fusion.4, f32[64,8]{0,1:T(8,128)S(1)} %fusion.126), channel_id=1, replica_groups=mesh['groups'=2,'prompt'=4,'enc'=4] {'prompt','enc'}, use_global_device_ids=true, to_apply=%region_4.6 | all-reduce | flops 8704 | bytes 69632 | tf_op jit(solution)/shard_map/psum | solution.py:179
  125.8 5.6 %all-reduce.1 = s32[32]{0:T(128)S(1)} all-reduce(s32[32]{0:T(128)S(1)} %dynamic-update-slice), channel_id=1, replica_groups=mesh['groups'=2,'prompt'=4,'enc'=4] {'prompt'}, use_global_device_ids=true, to_apply=%add.1 | all-reduce | flops 32 | bytes 256
  132.7 27.0 %reshape.370 = s32[64,2,2,64,2,2]{5,4,3,2,1,0:T(2,128)} reshape(s32[256,256]{1,0:T(8,128)S(1)} %copy-done.15) | data formatting | bytes 524288 | tf_op jit(solution)/shard_map/reshape | solution.py:49
  159.8 21.1 %copy.152 = s32[64,64,2,2,2,2]{1,0,5,4,3,2:T(8,128)S(1)} copy(s32[64,64,2,2,2,2]{5,3,1,4,2,0:T(2,128)} %bitcast.445) | data formatting | bytes 524288 | tf_op jit(solution)/shard_map/transpose | solution.py:50
  181.7 130.8 %while.15 = (s32[]{:T(128)}, f32[256,128]{0,1:T(8,128)S(1)}, f32[256,256]{0,1:T(8,128)S(1)}, f32[4,4,4,256]{3,2,1,0:T(4,128)}, f32[256,256]{0,1:T(8,128)S(1)}, /...) while((s32[]{:T(128)}, f32[256,128]{0,1:T(8,128)S(1)}, ...), condition=%wide.region_22.24_spmd.clone, body=%wide.region_9.23_spmd.clone.sunk | while | flops 716683264 | bytes 52255548 | solution.py:218
  181.9 1.1 fusion.330
  183.5 1.1 fusion.332
  185.8 1.1 bitcast_reduce_fusion.5
  187.1 3.7 fusion.339
  190.8 4.6 %multiply_multiply_fusion.19 = (f32[4,256,4,128]{1,3,2,0:T(8,128)S(1)}, f32[4,256,4,128]{1,3,2,0:T(8,128)S(1)}) fusion(f32[4,256,4,128]{1,3,2,0:T(8,128)S(1)} %get-tuple-element.461, u8[256,4,128]{0,2,1:T(8,128)(4,1)S(1)} %get-tuple-element.462), kind=kLoop, calls=%fused_computation.28.clone.1 | loop fusion | flops 35127296 | bytes 6422528 | tf_op jit(solution)/shard_map/while/body/eval_jaxpr/jvp(vmap())/mul | solution.py:103
  196.3 0.9 fusion.337
  197.1 1.2 fusion.340
  199.2 1.8 fusion.350
  203.2 0.9 fusion.343
  204.1 3.6 multiply_reduce_fusion.13
  208.5 1.0 multiply_reduce_fusion.14
  214.5 1.1 fusion.330
  216.2 1.1 fusion.332
  218.4 1.1 bitcast_reduce_fusion.5
  219.7 3.7 fusion.339
  223.4 4.6 %multiply_multiply_fusion.19 = (f32[4,256,4,128]{1,3,2,0:T(8,128)S(1)}, f32[4,256,4,128]{1,3,2,0:T(8,128)S(1)}) fusion(f32[4,256,4,128]{1,3,2,0:T(8,128)S(1)} %get-tuple-element.461, u8[256,4,128]{0,2,1:T(8,128)(4,1)S(1)} %get-tuple-element.462), kind=kLoop, calls=%fused_computation.28.clone.1 | loop fusion | flops 35127296 | bytes 6422528 | tf_op jit(solution)/shard_map/while/body/eval_jaxpr/jvp(vmap())/mul | solution.py:103
  228.9 0.9 fusion.337
  229.8 1.2 fusion.340
  231.8 1.8 fusion.350
  235.8 0.9 fusion.343
  236.7 3.6 multiply_reduce_fusion.13
  241.1 1.0 multiply_reduce_fusion.14
  247.1 1.1 fusion.330
  248.7 1.1 fusion.332
  251.0 1.1 bitcast_reduce_fusion.5
  252.3 3.7 fusion.339
  256.0 4.6 %multiply_multiply_fusion.19 = (f32[4,256,4,128]{1,3,2,0:T(8,128)S(1)}, f32[4,256,4,128]{1,3,2,0:T(8,128)S(1)}) fusion(f32[4,256,4,128]{1,3,2,0:T(8,128)S(1)} %get-tuple-element.461, u8[256,4,128]{0,2,1:T(8,128)(4,1)S(1)} %get-tuple-element.462), kind=kLoop, calls=%fused_computation.28.clone.1 | loop fusion | flops 35127296 | bytes 6422528 | tf_op jit(solution)/shard_map/while/body/eval_jaxpr/jvp(vmap())/mul | solution.py:103
  261.5 0.9 fusion.337
  262.4 1.2 fusion.340
  264.4 1.8 fusion.350
  268.4 0.9 fusion.343
  269.3 3.6 multiply_reduce_fusion.13
  273.7 1.0 multiply_reduce_fusion.14
  279.7 1.1 fusion.330
  281.4 1.1 fusion.332
  283.6 1.1 bitcast_reduce_fusion.5
  284.9 3.7 fusion.339
  288.6 4.6 %multiply_multiply_fusion.19 = (f32[4,256,4,128]{1,3,2,0:T(8,128)S(1)}, f32[4,256,4,128]{1,3,2,0:T(8,128)S(1)}) fusion(f32[4,256,4,128]{1,3,2,0:T(8,128)S(1)} %get-tuple-element.461, u8[256,4,128]{0,2,1:T(8,128)(4,1)S(1)} %get-tuple-element.462), kind=kLoop, calls=%fused_computation.28.clone.1 | loop fusion | flops 35127296 | bytes 6422528 | tf_op jit(solution)/shard_map/while/body/eval_jaxpr/jvp(vmap())/mul | solution.py:103
  294.1 0.9 fusion.337
  295.0 1.2 fusion.340
  297.0 1.8 fusion.350
  301.1 0.9 fusion.343
  301.9 3.6 multiply_reduce_fusion.13
  306.3 1.0 multiply_reduce_fusion.14
  312.6 1.5 reshape.372
  314.6 84.1 %all-reduce.5.cloned.1.call-done = f32[64,256]{1,0:T(8,128)} async-done(((f32[64,256]{1,0:T(8,128)}), f32[64,256]{1,0:T(8,128)}) %all-reduce.5.cloned.1.call-update) | async-done | bytes 65552 | tf_op jit(solution)/shard_map/psum | solution.py:227
  398.7 1.1 multiply_reduce_fusion.5
  400.4 1.1 fusion.167
  401.5 1.2 multiply_reduce_fusion.4
  402.7 1.2 fusion.128
  405.5 1.0 convolution_add_fusion.3
  (312 shorter events, 58.8 us)
Async XLA Ops:
  6.5 174.6 %copy-start = (bf16[256,128]{1,0:T(8,128)(2,1)S(1)}, bf16[256,128]{1,0:T(8,128)(2,1)}, u32[]{:S(2)}) copy-start(bf16[256,128]{1,0:T(8,128)(2,1)} %param.37) | copy-start | bytes 196612
  6.5 23.5 %copy-start.6 = (bf16[256,256]{1,0:T(8,128)(2,1)S(1)}, bf16[256,256]{1,0:T(8,128)(2,1)}, u32[]{:S(2)}) copy-start(bf16[256,256]{1,0:T(8,128)(2,1)} %param.26) | copy-start | bytes 393220
  6.5 23.6 %copy-start.17 = (bf16[256,128]{1,0:T(8,128)(2,1)S(1)}, bf16[256,128]{1,0:T(8,128)(2,1)}, u32[]{:S(2)}) copy-start(bf16[256,128]{1,0:T(8,128)(2,1)} %param.34) | copy-start | bytes 196612
  6.5 55.7 %copy-start.19 = (bf16[256,128]{1,0:T(8,128)(2,1)S(1)}, bf16[256,128]{1,0:T(8,128)(2,1)}, u32[]{:S(2)}) copy-start(bf16[256,128]{1,0:T(8,128)(2,1)} %param.35) | copy-start | bytes 196612
  6.5 392.1 %all-reduce.5.cloned.1.call-start = ((), (), s32[]{:S(2)}) async-start(), calls=%async_computation | async-start | bytes 131072 | tf_op jit(solution)/shard_map/psum | solution.py:227
  26.1 96.4 %copy-start.16 = (bf16[128,256]{1,0:T(8,128)(2,1)S(1)}, bf16[128,256]{1,0:T(8,128)(2,1)}, u32[]{:S(2)}) copy-start(bf16[128,256]{1,0:T(8,128)(2,1)} %param.36) | copy-start | bytes 196612
  28.9 94.6 %copy-start.25 = (f32[256]{0:T(256)S(1)}, f32[256]{0:T(256)}, u32[]{:S(2)}) copy-start(f32[256]{0:T(256)} %param.41) | copy-start | bytes 3076
  29.0 95.2 %copy-start.32 = (u32[32]{0:T(128)S(1)}, u32[32]{0:T(128)}, u32[]{:S(2)}) copy-start(u32[32]{0:T(128)} %constant.134) | copy-start | bytes 388
  29.0 96.5 %copy-start.31 = (s32[8]{0:T(128)S(1)}, s32[8]{0:T(128)}, u32[]{:S(2)}) copy-start(s32[8]{0:T(128)} %param.28) | copy-start | bytes 100
  30.1 102.6 %copy-start.15 = (s32[256,256]{1,0:T(8,128)S(1)}, s32[256,256]{1,0:T(8,128)}, u32[]{:S(2)}) copy-start(s32[256,256]{1,0:T(8,128)} %param.30) | copy-start | bytes 786436
  30.6 0.6 copy-start.11
  31.9 93.6 %copy-start.4 = (f32[64,8,256]{2,0,1:T(8,128)}, f32[64,8,256]{2,0,1:T(8,128)S(1)}, u32[]{:S(2)}) copy-start(f32[64,8,256]{2,0,1:T(8,128)S(1)} %get-tuple-element.321) | copy-start | bytes 1572868
  62.3 0.6 copy-start.23
  62.5 97.2 %copy-start.13 = (f32[256,128]{0,1:T(8,128)}, f32[256,128]{0,1:T(8,128)S(1)}, u32[]{:S(2)}) copy-start(f32[256,128]{0,1:T(8,128)S(1)} %fusion.180) | copy-start | bytes 393220
  121.8 37.9 %copy-start.27 = (f32[64,8]{0,1:T(8,128)}, f32[64,8]{0,1:T(8,128)S(1)}, u32[]{:S(2)}) copy-start(f32[64,8]{0,1:T(8,128)S(1)} %get-tuple-element.287) | copy-start | bytes 6148
  121.9 0.6 copy-start.10
  122.8 0.6 copy-start.7
  122.8 36.9 %copy-start.26 = (f32[64]{0:T(128)}, f32[64]{0:T(128)S(1)}, u32[]{:S(2)}) copy-start(f32[64]{0:T(128)S(1)} %broadcast_multiply_fusion.3) | copy-start | bytes 772
  123.0 36.7 %copy-start.30 = (f32[64]{0:T(128)}, f32[64]{0:T(128)S(1)}, u32[]{:S(2)}) copy-start(f32[64]{0:T(128)S(1)} %multiply_reduce_fusion.6) | copy-start | bytes 772
  123.4 36.3 %copy-start.29 = (f32[64]{0:T(128)}, f32[64]{0:T(128)S(1)}, u32[]{:S(2)}) copy-start(f32[64]{0:T(128)S(1)} %fusion.155) | copy-start | bytes 772
  159.8 21.6 %copy-start.21 = (bf16[256,128]{1,0:T(8,128)(2,1)S(1)}, bf16[256,128]{1,0:T(8,128)(2,1)}, u32[]{:S(2)}) copy-start(bf16[256,128]{1,0:T(8,128)(2,1)} %param.39) | copy-start | bytes 196612
  159.8 21.7 %copy-start.22 = (bf16[256,128]{1,0:T(8,128)(2,1)S(1)}, bf16[256,128]{1,0:T(8,128)(2,1)}, u32[]{:S(2)}) copy-start(bf16[256,128]{1,0:T(8,128)(2,1)} %param.38) | copy-start | bytes 196612
  159.8 21.9 %copy-start.1 = (bf16[256,256]{1,0:T(8,128)(2,1)S(1)}, bf16[256,256]{1,0:T(8,128)(2,1)}, u32[]{:S(2)}) copy-start(bf16[256,256]{1,0:T(8,128)(2,1)} %param.44) | copy-start | bytes 393220
  159.8 21.9 %copy-start.2 = (bf16[256,256]{1,0:T(8,128)(2,1)S(1)}, bf16[256,256]{1,0:T(8,128)(2,1)}, u32[]{:S(2)}) copy-start(bf16[256,256]{1,0:T(8,128)(2,1)} %param.46) | copy-start | bytes 393220
  159.8 21.9 %copy-start.3 = (bf16[128,256]{1,0:T(8,128)(2,1)S(1)}, bf16[128,256]{1,0:T(8,128)(2,1)}, u32[]{:S(2)}) copy-start(bf16[128,256]{1,0:T(8,128)(2,1)} %param.40) | copy-start | bytes 196612
  181.7 221.0 %copy-start.5 = (f32[64,8,256]{2,0,1:T(8,128)S(1)}, f32[64,8,256]{2,0,1:T(8,128)}, u32[]{:S(2)}) copy-start(f32[64,8,256]{2,0,1:T(8,128)} %copy-done.4) | copy-start | bytes 1572868
  209.8 0.6 copy-start.8
  211.4 2.5 copy-start.9
  242.4 0.6 copy-start.8
  244.0 2.5 copy-start.9
  275.0 0.6 copy-start.8
  276.6 2.5 copy-start.9
  307.6 0.6 copy-start.8
  309.2 2.5 copy-start.9
  312.5 91.5 %copy-start.14 = (f32[256,128]{0,1:T(8,128)S(1)}, f32[256,128]{0,1:T(8,128)}, u32[]{:S(2)}) copy-start(f32[256,128]{0,1:T(8,128)} %copy-done.13) | copy-start | bytes 393220
  312.5 91.5 %copy-start.24 = (f32[64,8]{0,1:T(8,128)S(1)}, f32[64,8]{0,1:T(8,128)}, u32[]{:S(2)}) copy-start(f32[64,8]{0,1:T(8,128)} %copy-done.23) | copy-start | bytes 6148
  312.5 91.5 %copy-start.28 = (f32[64,8]{0,1:T(8,128)S(1)}, f32[64,8]{0,1:T(8,128)}, u32[]{:S(2)}) copy-start(f32[64,8]{0,1:T(8,128)} %copy-done.27) | copy-start | bytes 6148
  402.7 2.1 copy-start.12
  402.7 2.5 copy-start.18
  404.0 1.5 copy-start.20
Sparse Core Ops, SparseCore 0:
  314.2 84.3 all-reduce.4
